TPU v7x, 32 devices: a whole 2x2x4 slice. The times are simulated.
32 devices in a mesh: dp: 4 (over z), expert: 8 (over y, x, core).
Axes of the slice: x: 2, y: 2, z: 4, core: 2. Of those that a mesh axis runs over, the one named last changes fastest.
Arguments:
- hidden: bfloat16 [3072, 2880], P('expert', 'dp'), may hold values from -6 to 6
- segments: int32 [8, 384], P('expert'), may hold values from 0 to 3, never falling along the last dimension, each value on 1 to 192 neighbouring positions
- request_adapter: int32 [8, 4], P('expert'), may hold values from 0 to 7
- routes: int32 [8, 384, 4], P('expert', 'dp'), may hold values from 0 to 7, all different within a row; in each aligned block of 96 rows (0 to 95, 96 to 191, ..., all dimensions but the last counted through in order) at most 64 rows name the same one
- expert_gates: bfloat16 [8, 384, 4], P('expert', 'dp'), may hold values from 0.049804688 to 0.59765625
- attention_gain: float32 [2880], replicated, may hold values from 0.25 to 1.75
- joined_weight: bfloat16 [2880, 4, 640], P(None, 'dp'), may hold values from -0.109375 to 0.109375
- sinks: float32 [32], P('dp'), may hold values from 0 to 3
- attention_out_weight: bfloat16 [2048, 2880], P('dp'), may hold values from -0.125 to 0.125
- joined_down_maps: bfloat16 [2880, 128], replicated, may hold values from -0.109375 to 0.109375
- joined_up_maps: bfloat16 [128, 4, 640], P(None, 'dp'), may hold values from -0.375 to 0.375
- output_down_maps: bfloat16 [2048, 128], P('dp'), may hold values from -0.125 to 0.125
- output_up_maps: bfloat16 [128, 2880], P(None, 'dp'), may hold values from -0.75 to 0.75
- expert_norm_gain: float32 [2880], replicated, may hold values from 0.25 to 1.75
- expert_gate_weight: bfloat16 [8, 2880, 2880], P('expert', None, 'dp'), may hold values from -0.109375 to 0.109375
- expert_up_weight: bfloat16 [8, 2880, 2880], P('expert', None, 'dp'), may hold values from -0.109375 to 0.109375
- expert_down_weight: bfloat16 [8, 2880, 2880], P('expert', 'dp'), may hold values from -0.109375 to 0.109375
- closing_gain: float32 [2880], replicated, may hold values from 0.25 to 1.75
- vocabulary_weight: bfloat16 [2880, 25600], P(None, ('dp', 'expert')), may hold values from -0.109375 to 0.109375
Outputs:
- hidden_out: bfloat16 [3072, 2880], P('expert', 'dp')
- logits: float32 [32, 25600], P(None, ('dp', 'expert'))
Inputs may be any that keep to these rules, and one draw needn't show every extreme that they name: `segments`: in each column the ids do not fall; each of the 4 requests has 1 to 192 tokens, and one has exactly 192. `routes`: the 4 experts of a token differ. Within the rows of one device (96 consecutive tokens, aligned blocks) no expert is named more than 64 times, and in some blocks one expert is named exactly 64 times.
All inputs are finite; a program needn't handle non-finite values.
Results may differ from a plain program's by a relative error of at most 0.02.
Values may be sent and summed in bfloat16 or wider, within the bound.
No kernel may reach another device: no remote copies, remote signals or barrier semaphores. Data moves between devices by JAX's collectives and lax.ppermute only.
A program may use at most 128 MiB of HBM per device.

v0:
```python
import jax
import jax.numpy as jnp
from jax import lax
from jax.sharding import PartitionSpec as P

HEAD_SIZE = 64
QUERY_GROUP = 8
TOP = 4
ADAPTER_RANK = 16
REQS = 4
epsilon = 1e-05
theta_base = 150000.0
adapter_scale = 2.0
glu_alpha = 1.702


def rms_scale(values, gain_row):
    mean_square = jnp.mean(values * values, axis=-1, keepdims=True)
    return values * lax.rsqrt(mean_square + epsilon) * gain_row


def positions_of(segment_row):
    counter = jnp.arange(segment_row.shape[0], dtype=jnp.int32)
    starting = jnp.concatenate(
        [jnp.ones((1,), dtype=jnp.bool_), segment_row[1:] != segment_row[:-1]]
    )
    first_index = lax.cummax(jnp.where(starting, counter, 0), axis=0)
    return counter - first_index


def adapter_per_token(segment_row, adapter_row):
    hits = segment_row[:, None] == jnp.arange(adapter_row.shape[0], dtype=jnp.int32)[None, :]
    return jnp.sum(jnp.where(hits, adapter_row[None, :], 0), axis=1)


def rotate_heads(values, positions):
    head_dim = values.shape[-1]
    half_dim = head_dim // 2
    frequency = theta_base ** (-2.0 * jnp.arange(half_dim, dtype=jnp.float32) / head_dim)
    angles = positions.astype(jnp.float32)[:, None] * frequency[None, :]
    cosine = jnp.cos(angles)[:, None, :]
    sine_part = jnp.sin(angles)[:, None, :]
    first_half = values[..., :half_dim]
    second_half = values[..., half_dim:]
    return jnp.concatenate(
        [
            first_half * cosine - second_half * sine_part,
            second_half * cosine + first_half * sine_part,
        ],
        axis=-1,
    )


def attend_heads(queries, key_heads, value_heads, segment_row, sink_row):
    tokens_now, kv_now, group_now, head_dim = queries.shape
    scores = jnp.einsum(
        "tkgh,skh->kgts", queries, key_heads, preferred_element_type=jnp.float32
    ) * head_dim ** (-0.5)
    counter = jnp.arange(tokens_now, dtype=jnp.int32)
    allowed = (segment_row[:, None] == segment_row[None, :]) & (
        counter[None, :] <= counter[:, None]
    )
    weights = jnp.where(allowed[None, None], jnp.exp(scores), 0.0)
    totals = jnp.sum(weights, axis=-1, keepdims=True) + jnp.exp(sink_row).reshape(
        kv_now, group_now, 1, 1
    )
    probs = (weights / totals).astype(jnp.bfloat16)
    blended_hidden = jnp.einsum(
        "kgts,skh->tkgh", probs, value_heads, preferred_element_type=jnp.float32
    )
    return blended_hidden.astype(jnp.bfloat16).reshape(tokens_now, kv_now * group_now * head_dim)


def shards(
    hidden,
    segments,
    request_adapter,
    routes,
    expert_gates,
    attention_gain,
    joined_weight,
    sinks,
    attention_out_weight,
    joined_down_maps,
    joined_up_maps,
    output_down_maps,
    output_up_maps,
    expert_norm_gain,
    expert_gate_weight,
    expert_up_weight,
    expert_down_weight,
    closing_gain,
    vocabulary_weight,
):
    groups = lax.axis_size("dp")
    columns = lax.axis_size("expert")
    position_dp = lax.axis_index("dp")
    segment_row = segments[0]
    adapter_row = request_adapter[0]
    col_tokens = segment_row.shape[0]
    gathered_rows = lax.all_gather(hidden, "dp", axis=1, tiled=True)
    width = gathered_rows.shape[1]
    normalized_hidden = rms_scale(gathered_rows.astype(jnp.float32), attention_gain).astype(
        jnp.bfloat16
    )
    joined_projection = jnp.dot(
        normalized_hidden, joined_weight.reshape(width, -1), preferred_element_type=jnp.float32
    )
    reduced_every_adapter = joined_down_maps.shape[1]
    reduced_hidden = jnp.dot(
        normalized_hidden, joined_down_maps, preferred_element_type=jnp.float32
    ).astype(jnp.bfloat16)
    rank_owner = jnp.arange(reduced_every_adapter, dtype=jnp.int32) // ADAPTER_RANK
    adapter_mask = adapter_per_token(segment_row, adapter_row)[:, None] == rank_owner[None, :]
    selected_reduced = jnp.where(adapter_mask, reduced_hidden, jnp.zeros_like(reduced_hidden))
    joined_projection = joined_projection + adapter_scale * jnp.dot(
        selected_reduced,
        joined_up_maps.reshape(reduced_every_adapter, -1),
        preferred_element_type=jnp.float32,
    )
    kv_here = joined_weight.shape[1]
    joined_projection = joined_projection.reshape(col_tokens, kv_here, QUERY_GROUP + 2, HEAD_SIZE)
    positions = positions_of(segment_row)
    queries = rotate_heads(
        joined_projection[:, :, :QUERY_GROUP].reshape(col_tokens, kv_here * QUERY_GROUP, HEAD_SIZE),
        positions,
    )
    queries = queries.astype(jnp.bfloat16).reshape(col_tokens, kv_here, QUERY_GROUP, HEAD_SIZE)
    key_heads = rotate_heads(joined_projection[:, :, QUERY_GROUP], positions).astype(jnp.bfloat16)
    value_heads = joined_projection[:, :, QUERY_GROUP + 1].astype(jnp.bfloat16)
    blended_hidden = attend_heads(queries, key_heads, value_heads, segment_row, sinks)
    share = col_tokens // groups
    quarter = hidden.shape[1]
    rank_total = output_down_maps.shape[1]
    route_pack = jnp.concatenate(
        [routes[0].astype(jnp.bfloat16), expert_gates[0].astype(jnp.bfloat16)], axis=1
    )
    pack_width = -(quarter + rank_total) % 128 or 128
    route_pack = jnp.pad(route_pack, ((0, 0), (0, pack_width - 2 * TOP)))
    pack_rows = lax.dynamic_update_slice_in_dim(
        jnp.zeros((col_tokens, pack_width), jnp.bfloat16), route_pack, position_dp * share, 0
    )
    partial_out = jnp.dot(blended_hidden, attention_out_weight, preferred_element_type=jnp.float32)
    low_local = jnp.dot(blended_hidden, output_down_maps, preferred_element_type=jnp.float32)
    joined_send = jnp.concatenate(
        [
            partial_out.astype(jnp.bfloat16).reshape(col_tokens, groups, quarter),
            jnp.broadcast_to(
                low_local.astype(jnp.bfloat16)[:, None, :], (col_tokens, groups, rank_total)
            ),
            jnp.broadcast_to(pack_rows[:, None, :], (col_tokens, groups, pack_width)),
        ],
        axis=2,
    ).reshape(col_tokens, -1)
    reduced_parts = []

    def reduce_rows(lo, rows):
        joined_back = lax.psum_scatter(
            joined_send[lo : lo + rows], "dp", scatter_dimension=1, tiled=True
        )
        return joined_back

    def resid_rows(joined_back, lo, rows):
        mine_out = joined_back[:, :quarter].astype(jnp.float32)
        output_reduced = joined_back[:, quarter : quarter + rank_total]
        selected_output = jnp.where(
            adapter_mask[lo : lo + rows], output_reduced, jnp.zeros_like(output_reduced)
        )
        adapter_delta = adapter_scale * jnp.dot(
            selected_output, output_up_maps, preferred_element_type=jnp.float32
        )
        resid_part = (hidden[lo : lo + rows].astype(jnp.float32) + mine_out + adapter_delta).astype(
            jnp.bfloat16
        )
        return (resid_part, joined_back[:, quarter + rank_total :])

    lane_pad = -width % 128
    wide = width + lane_pad
    experts = expert_gate_weight.shape[0] * columns
    capacity = 4 * share * TOP // (3 * experts)
    gate_weight = expert_gate_weight[0]
    up_weight = expert_up_weight[0]
    down_weight = jnp.pad(expert_down_weight[0], ((0, 0), (0, lane_pad)))
    halves = 2 if groups % 2 == 0 else 1
    half_tokens = col_tokens // halves
    half_capacity = groups // halves * capacity
    counter = jnp.arange(col_tokens, dtype=jnp.int32)
    request_ids = jnp.arange(REQS, dtype=jnp.int32)
    last_index = jnp.max(
        jnp.where(segment_row[None, :] == request_ids[:, None], counter[None, :], -1), axis=1
    )
    last_index = jnp.clip(last_index, 0, col_tokens - 1)
    moe_rows = []
    last_parts = []
    last_resid_parts = []
    held = None
    pending = None
    for h in range(halves):
        lo = h * half_tokens
        joined_h = reduce_rows(lo, half_tokens)
        resid_h, pack_h = resid_rows(joined_h, lo, half_tokens)
        reduced_parts.append(resid_h)
        column_h = lax.all_gather(resid_h, "dp", axis=1, tiled=True)
        if held is not None:
            column_h, held = lax.optimization_barrier((column_h, held))
        moe_in = rms_scale(column_h.astype(jnp.float32), expert_norm_gain).astype(jnp.bfloat16)
        moe_in = jnp.pad(moe_in, ((0, 0), (0, lane_pad)))
        route_flat = pack_h[:, :TOP].astype(jnp.int32).reshape(-1)
        gates_h = pack_h[:, TOP : 2 * TOP]
        one_hot = (route_flat[:, None] == jnp.arange(experts, dtype=jnp.int32)[None, :]).astype(
            jnp.int32
        )
        slot_rows = jnp.sum((jnp.cumsum(one_hot, axis=0) - one_hot) * one_hot, axis=1)
        target = route_flat * half_capacity + slot_rows
        source_rows = jnp.arange(route_flat.shape[0], dtype=jnp.int32) // TOP
        table = (
            jnp.full((experts * half_capacity,), half_tokens, jnp.int32).at[target].set(source_rows)
        )
        dispatch = (table[:, None] == jnp.arange(half_tokens, dtype=jnp.int32)[None, :]).astype(
            jnp.bfloat16
        )
        outgoing = (
            jnp.dot(dispatch, moe_in, preferred_element_type=jnp.float32)
            .astype(jnp.bfloat16)
            .reshape(experts, half_capacity, wide)
        )
        arrived = lax.all_to_all(outgoing, "expert", split_axis=0, concat_axis=0, tiled=True)
        if h == 0:
            held = arrived
        else:
            arrived = lax.optimization_barrier((arrived, held))[0]
        rows_in = arrived.reshape(-1, wide)[:, :width]
        gate_part = jnp.dot(rows_in, gate_weight, preferred_element_type=jnp.float32)
        up_part = jnp.dot(rows_in, up_weight, preferred_element_type=jnp.float32)
        activated = (gate_part * jax.nn.sigmoid(glu_alpha * gate_part) * (up_part + 1.0)).astype(
            jnp.bfloat16
        )
        shares_out = (
            jnp.dot(activated, down_weight, preferred_element_type=jnp.float32)
            .astype(jnp.bfloat16)
            .reshape(experts, half_capacity, wide)
        )
        answers = lax.all_to_all(shares_out, "expert", split_axis=0, concat_axis=0, tiled=True)
        if pending is not None:
            moe_rows.append(lax.psum_scatter(pending, "dp", scatter_dimension=1, tiled=True))
            answers, moe_rows[-1] = lax.optimization_barrier((answers, moe_rows[-1]))
            pending = None
        slot_ids = jnp.arange(experts * half_capacity, dtype=jnp.int32)
        combine = jnp.sum(
            jnp.where(
                target.reshape(half_tokens, TOP)[:, :, None] == slot_ids[None, None, :],
                gates_h[:, :, None],
                jnp.zeros((), jnp.bfloat16),
            ),
            axis=1,
        ).astype(jnp.bfloat16)
        mixture = jnp.dot(
            combine,
            answers.reshape(experts * half_capacity, wide),
            preferred_element_type=jnp.float32,
        )[:, :width]
        local_last = jnp.clip(last_index - lo, 0, half_tokens - 1)
        inside = ((last_index >= lo) & (last_index < lo + half_tokens))[:, None]
        last_parts.append(
            jnp.where(inside, jnp.take(mixture, local_last, axis=0), jnp.zeros((), jnp.float32))
        )
        last_resid_parts.append(
            jnp.where(inside, jnp.take(column_h, local_last, axis=0), jnp.zeros((), jnp.bfloat16))
        )
        if h < halves - 1:
            pending = mixture.astype(jnp.bfloat16)
        else:
            last_mix = sum(last_parts).reshape(REQS * groups, quarter)
            moe_send = jnp.concatenate([mixture, jnp.tile(last_mix, (1, groups))], axis=0).astype(
                jnp.bfloat16
            )
            moe_rows.append(lax.psum_scatter(moe_send, "dp", scatter_dimension=1, tiled=True))
    moe_back = jnp.concatenate(moe_rows, axis=0)
    moe_rounded = moe_back[:col_tokens].astype(jnp.float32).astype(jnp.bfloat16)
    resid = jnp.concatenate(reduced_parts, axis=0)
    hidden_out = (resid.astype(jnp.float32) + moe_rounded.astype(jnp.float32)).astype(jnp.bfloat16)
    last_moe = moe_back[col_tokens:].reshape(REQS, width)
    last_resid = sum((part.astype(jnp.float32) for part in last_resid_parts))
    last_hidden = (last_resid + last_moe.astype(jnp.float32)).astype(jnp.bfloat16)
    ends = rms_scale(last_hidden.astype(jnp.float32), closing_gain).astype(jnp.bfloat16)
    tail_rows = lax.all_gather(ends, "expert", axis=0, tiled=True)
    logits = jnp.dot(tail_rows, vocabulary_weight, preferred_element_type=jnp.float32)
    return (hidden_out, logits)


def solution(mesh):
    in_specs = (
        P("expert", "dp"),
        P("expert", None),
        P("expert", None),
        P("expert", "dp", None),
        P("expert", "dp", None),
        P(),
        P(None, "dp", None),
        P("dp"),
        P("dp", None),
        P(),
        P(None, "dp", None),
        P("dp", None),
        P(None, "dp"),
        P(),
        P("expert", None, "dp"),
        P("expert", None, "dp"),
        P("expert", "dp", None),
        P(),
        P(None, ("dp", "expert")),
    )
    out_specs = (P("expert", "dp"), P(None, ("dp", "expert")))
    return jax.shard_map(shards, mesh=mesh, in_specs=in_specs, out_specs=out_specs, check_vma=False)
```

profile of v0, /device:TPU:0, one launch (start us, length us, event | category | flops | bytes accessed | tf_op | source)
XLA Modules:
  0.0 549.6 jit_solution(267624168265766925)
XLA Ops:
  13.7 46.6 %all-gather.7.cloned.1.call-done = bf16[384,2880]{0,1:T(8,128)(2,1)} async-done(((bf16[384,720]{0,1:T(8,128)(2,1)}), bf16[384,2880]{0,1:T(8,128)(2,1)}) %all-gather.7.cloned.1.call-update) | async-done | bytes 2211856 | tf_op jit(solution)/shard_map/all_gather | solution.py:101
  60.4 2.2 fusion.12
  62.6 5.9 %fusion.22 = f32[384,640]{1,0:T(8,128)} fusion(bf16[2880,1,640]{2,0,1:T(8,128)(2,1)} %param.29, bf16[384,2880]{0,1:T(8,128)(2,1)} %all-gather.7.cloned.1.call-done, f32[2880]{0:T(1024)S(1)} %copy-done.16, f32[384]{0:T(512)S(1)} %add_rsqrt_fusion), kind=kOutput, calls=%fused_computation.37 | convolution fusion | flops 1420001280 | bytes 6894336 | tf_op jit(solution)/shard_map/dot_general | solution.py:106
  68.5 4.8 fusion.56
  73.3 2.5 copy.64
  76.7 1.2 slice_bitcast_fusion
  78.3 1.3 fusion.19
  79.6 2.2 fusion.59
  82.4 1.7 convolution_convert_fusion.4
  84.4 2.9 fusion.136
  88.4 37.4 %reduce-scatter.13.cloned.1.call-done = bf16[896,192]{1,0:T(8,128)(2,1)} async-done(((bf16[3584,192]{1,0:T(8,128)(2,1)}), bf16[896,192]{1,0:T(8,128)(2,1)}) %reduce-scatter.13.cloned.1.call-update) | async-done | bytes 344080
  130.1 1.7 reduce-window.29
  132.7 3.4 scatter_custom_fusion.1
  136.1 22.6 %all-gather.11.cloned.1.call-done = bf16[4,720,192]{1,2,0:T(8,128)(2,1)} async-done(((bf16[1,720,192]{1,2,0:T(8,128)(2,1)}), bf16[4,720,192]{1,2,0:T(8,128)(2,1)}) %all-gather.11.cloned.1.call-update) | async-done | bytes 1105936 | tf_op jit(solution)/shard_map/all_gather | solution.py:203
  158.6 2.2 copy.75
  162.5 4.5 convolution_convert_fusion.1
  166.9 4.7 all-to-all-start
  172.5 41.0 %reduce-scatter.15.cloned.1.call-done = bf16[896,192]{1,0:T(8,128)(2,1)} async-done(((bf16[3584,192]{1,0:T(8,128)(2,1)}), bf16[896,192]{1,0:T(8,128)(2,1)}) %reduce-scatter.15.cloned.1.call-update) | async-done | bytes 344080
  217.8 1.7 reduce-window.25
  220.4 3.6 scatter_custom_fusion
  223.9 22.4 %all-gather.9.cloned.1.call-done = bf16[4,720,192]{1,2,0:T(8,128)(2,1)} async-done(((bf16[1,720,192]{1,2,0:T(8,128)(2,1)}), bf16[4,720,192]{1,2,0:T(8,128)(2,1)}) %all-gather.9.cloned.1.call-update) | async-done | bytes 1105936 | tf_op jit(solution)/shard_map/all_gather | solution.py:203
  246.4 3.2 copy.72
  249.6 2.7 reshape.552
  253.0 4.4 convolution_convert_fusion
  257.4 4.7 all-to-all-start.1
  262.1 10.4 %fusion.4 = f32[1024,720]{0,1:T(8,128)} fusion(bf16[1024,2944]{1,0:T(8,128)(2,1)} %bitcast.45, bf16[1,2880,720]{1,2,0:T(8,128)(2,1)} %param.38), kind=kOutput, calls=%fused_computation.16 | convolution fusion | flops 4246732800 | bytes 13125632 | tf_op jit(solution)/shard_map/dot_general | solution.py:234
  272.5 16.8 %convolution_convert_fusion.2 = bf16[1024,2944]{1,0:T(8,128)(2,1)} fusion(bf16[720,2880]{1,0:T(8,128)(2,1)} %bitcast.183, f32[1024,720]{0,1:T(8,128)} %fusion.4, bf16[1,2880,720]{1,2,0:T(8,128)(2,1)} %param.37, bf16[1024,2944]{1,0:T(8,128)(2,1)} %bitcast.45), kind=kOutput, calls=%fused_computation.12 | convolution fusion | flops 8596750336 | bytes 23302144 | tf_op jit(solution)/shard_map/dot_general | solution.py:239
  289.3 41.6 %all-to-all-done.1 = bf16[8,128,2944]{2,1,0:T(8,128)(2,1)} async-done(((bf16[8,128,2944]{2,1,0:T(8,128)(2,1)}), bf16[8,128,2944]{2,1,0:T(8,128)(2,1)}, u32[]{:S(2)}, u32[]{:S(2)}) %all-to-all-start.1) | async-done | bytes 6029344 | tf_op jit(solution)/shard_map/all_to_all | solution.py:227
  330.9 4.9 all-to-all-start.3
  335.8 10.4 %fusion.8 = f32[1024,720]{0,1:T(8,128)} fusion(bf16[1024,2944]{1,0:T(8,128)(2,1)} %bitcast.40, bf16[1,2880,720]{1,2,0:T(8,128)(2,1)} %param.38), kind=kOutput, calls=%fused_computation.20 | convolution fusion | flops 4246732800 | bytes 13125632 | tf_op jit(solution)/shard_map/dot_general | solution.py:234
  346.2 16.8 %convolution_convert_fusion.3 = bf16[1024,2944]{1,0:T(8,128)(2,1)} fusion(bf16[720,2880]{1,0:T(8,128)(2,1)} %bitcast.184, f32[1024,720]{0,1:T(8,128)} %fusion.8, bf16[1,2880,720]{1,2,0:T(8,128)(2,1)} %param.37, bf16[1024,2944]{1,0:T(8,128)(2,1)} %bitcast.40), kind=kOutput, calls=%fused_computation.13 | convolution fusion | flops 8596750336 | bytes 23302144 | tf_op jit(solution)/shard_map/dot_general | solution.py:239
  363.0 41.6 %all-to-all-done.3 = bf16[8,128,2944]{2,1,0:T(8,128)(2,1)} async-done(((bf16[8,128,2944]{2,1,0:T(8,128)(2,1)}), bf16[8,128,2944]{2,1,0:T(8,128)(2,1)}, u32[]{:S(2)}, u32[]{:S(2)}) %all-to-all-start.3) | async-done | bytes 6029344 | tf_op jit(solution)/shard_map/all_to_all | solution.py:243
  404.6 4.7 all-to-all-start.2
  409.9 5.8 %fusion.140 = (bf16[192,2880]{1,0:T(8,128)(2,1)}, f32[192,2880]{1,0:T(8,128)}) fusion(bf16[192,1024]{1,0:T(8,128)(2,1)S(1)} %fusion.51, bf16[1024,2944]{1,0:T(8,128)(2,1)} %bitcast.47), kind=kOutput, calls=%fused_computation.218 | convolution fusion | flops 1133015040 | bytes 9740288 | tf_op jit(solution)/shard_map/dot_general | solution.py:257
  415.7 2.5 copy.88
  419.1 2.2 gather_fusion
  421.3 30.4 %reduce-scatter.17.cloned.1.call-done = bf16[720,192]{1,0:T(8,128)(2,1)} async-done(((bf16[2880,192]{1,0:T(8,128)(2,1)}), bf16[720,192]{1,0:T(8,128)(2,1)}) %reduce-scatter.17.cloned.1.call-update) | async-done | bytes 276496
  451.7 1.8 copy.89
  453.6 24.6 %all-to-all-done.2 = bf16[8,128,2944]{2,1,0:T(8,128)(2,1)} async-done(((bf16[8,128,2944]{2,1,0:T(8,128)(2,1)}), bf16[8,128,2944]{2,1,0:T(8,128)(2,1)}, u32[]{:S(2)}, u32[]{:S(2)}) %all-to-all-start.2) | async-done | bytes 6029344 | tf_op jit(solution)/shard_map/all_to_all | solution.py:243
  478.2 5.8 %fusion.141 = (bf16[192,2880]{1,0:T(8,128)(2,1)}, f32[192,2880]{1,0:T(8,128)}) fusion(bf16[192,1024]{1,0:T(8,128)(2,1)S(1)} %fusion.50, bf16[1024,2944]{1,0:T(8,128)(2,1)} %bitcast.48), kind=kOutput, calls=%fused_computation.219 | convolution fusion | flops 1133015040 | bytes 9740288 | tf_op jit(solution)/shard_map/dot_general | solution.py:257
  484.0 2.2 gather_fusion.1
  486.6 2.4 pad_maximum_fusion.1
  489.0 2.6 copy.90
  491.6 1.2 gather_fusion.2
  492.8 1.2 gather_fusion.3
  494.0 28.9 %reduce-scatter.19.cloned.1.call-done = bf16[720,208]{1,0:T(8,128)(2,1)} async-done(((bf16[2880,208]{1,0:T(8,128)(2,1)}), bf16[720,208]{1,0:T(8,128)(2,1)}) %reduce-scatter.19.cloned.1.call-update) | async-done | bytes 299536
  528.8 9.2 %all-gather.2 = bf16[8,4,2880]{2,1,0:T(4,128)(2,1)S(1)} all-gather(bf16[1,4,2880]{2,1,0:T(4,128)(2,1)S(1)} %fusion.108), channel_id=1, replica_groups=mesh['dp'=4,'expert'=8] {'expert'}, dimensions={0}, use_global_device_ids=true | all-gather | bytes 207360 | tf_op jit(solution)/shard_map/all_gather | solution.py:286
  538.1 4.4 fusion.142
  (149 shorter events, 30.5 us)
Async XLA Ops:
  7.2 75.2 %copy-start = (bf16[512,2880]{0,1:T(8,128)(2,1)S(1)}, bf16[512,2880]{0,1:T(8,128)(2,1)}, u32[]{:S(2)}) copy-start(bf16[512,2880]{0,1:T(8,128)(2,1)} %param.31) | copy-start | bytes 8847364
  7.2 55.4 %copy-start.16 = (f32[2880]{0:T(1024)S(1)}, f32[2880]{0:T(1024)}, u32[]{:S(2)}) copy-start(f32[2880]{0:T(1024)} %param.28) | copy-start | bytes 34564
  7.2 53.2 %all-gather.7.cloned.1.call-start = ((), (), s32[]{:S(2)}) async-start(), calls=%async_computation.8 | async-start | bytes 2764800 | tf_op jit(solution)/shard_map/all_gather | solution.py:101
  7.9 117.9 %reduce-scatter.13.cloned.1.call-start = ((), (), s32[]{:S(2)}) async-start(), calls=%async_computation.11 | async-start | bytes 2293760
  12.4 0.9 copy-start.7
  62.6 5.9 %copy-start.15 = (bf16[128,1,640]{2,0,1:T(8,128)(2,1)S(1)}, bf16[128,1,640]{2,0,1:T(8,128)(2,1)}, u32[]{:S(2)}) copy-start(bf16[128,1,640]{2,0,1:T(8,128)(2,1)} %param.33) | copy-start | bytes 491524
  79.6 2.3 copy-start.9
  82.3 1.7 copy-start.8
  84.4 3.5 copy-start.2
  87.4 40.6 %copy-start.5 = (bf16[128,720]{0,1:T(8,128)(2,1)S(1)}, bf16[128,720]{0,1:T(8,128)(2,1)}, u32[]{:S(2)}) copy-start(bf16[128,720]{0,1:T(8,128)(2,1)} %param.35) | copy-start | bytes 552964
  87.4 71.3 %all-gather.11.cloned.1.call-start = ((), (), s32[]{:S(2)}) async-start(), calls=%async_computation.10 | async-start | bytes 1474560 | tf_op jit(solution)/shard_map/all_gather | solution.py:203
  132.5 29.6 %copy-start.10 = (f32[2880]{0:T(1024)S(1)}, f32[2880]{0:T(1024)}, u32[]{:S(2)}) copy-start(f32[2880]{0:T(1024)} %param.36) | copy-start | bytes 34564
  166.9 85.3 %all-to-all-start = ((bf16[8,128,2944]{2,1,0:T(8,128)(2,1)}), bf16[8,128,2944]{2,1,0:T(8,128)(2,1)}, u32[]{:S(2)}, u32[]{:S(2)}) async-start(bf16[8,128,2944]{2,1,0:T(8,128)(2,1)} %bitcast.149), calls=%async_computation | async-start | bytes 12058624 | tf_op jit(solution)/shard_map/all_to_all | solution.py:227
  171.7 44.0 %copy-start.6 = (bf16[128,720]{0,1:T(8,128)(2,1)S(1)}, bf16[128,720]{0,1:T(8,128)(2,1)}, u32[]{:S(2)}) copy-start(bf16[128,720]{0,1:T(8,128)(2,1)} %param.35) | copy-start | bytes 552964
  171.7 41.8 %reduce-scatter.15.cloned.1.call-start = ((), (), s32[]{:S(2)}) async-start(), calls=%async_computation.12 | async-start | bytes 2293760
  172.3 74.1 %all-gather.9.cloned.1.call-start = ((), (), s32[]{:S(2)}) async-start(), calls=%async_computation.9 | async-start | bytes 1474560 | tf_op jit(solution)/shard_map/all_gather | solution.py:203
  257.4 73.5 %all-to-all-start.1 = ((bf16[8,128,2944]{2,1,0:T(8,128)(2,1)}), bf16[8,128,2944]{2,1,0:T(8,128)(2,1)}, u32[]{:S(2)}, u32[]{:S(2)}) async-start(bf16[8,128,2944]{2,1,0:T(8,128)(2,1)} %bitcast.150), calls=%async_computation.1 | async-start | bytes 12058624 | tf_op jit(solution)/shard_map/all_to_all | solution.py:227
  330.9 73.7 %all-to-all-start.3 = ((bf16[8,128,2944]{2,1,0:T(8,128)(2,1)}), bf16[8,128,2944]{2,1,0:T(8,128)(2,1)}, u32[]{:S(2)}, u32[]{:S(2)}) async-start(bf16[8,128,2944]{2,1,0:T(8,128)(2,1)} %bitcast.158), calls=%async_computation.3 | async-start | bytes 12058624 | tf_op jit(solution)/shard_map/all_to_all | solution.py:243
  404.6 73.5 %all-to-all-start.2 = ((bf16[8,128,2944]{2,1,0:T(8,128)(2,1)}), bf16[8,128,2944]{2,1,0:T(8,128)(2,1)}, u32[]{:S(2)}, u32[]{:S(2)}) async-start(bf16[8,128,2944]{2,1,0:T(8,128)(2,1)} %bitcast.157), calls=%async_computation.2 | async-start | bytes 12058624 | tf_op jit(solution)/shard_map/all_to_all | solution.py:243
  409.4 42.4 %reduce-scatter.17.cloned.1.call-start = ((), (), s32[]{:S(2)}) async-start(), calls=%async_computation.13 | async-start | bytes 1843200
  418.3 104.5 %reduce-scatter.19.cloned.1.call-start = ((), (), s32[]{:S(2)}) async-start(), calls=%async_computation.14 | async-start | bytes 1843200
  418.5 67.7 %copy-start.12 = (pred[4]{0:T(512)(128)(4,1)}, pred[4]{0:T(512)(128)(4,1)S(1)}, u32[]{:S(2)}) copy-start(pred[4]{0:T(512)(128)(4,1)S(1)} %get-tuple-element.42) | copy-start | bytes 16
  418.5 67.7 %copy-start.13 = (pred[4]{0:T(512)(128)(4,1)}, pred[4]{0:T(512)(128)(4,1)S(1)}, u32[]{:S(2)}) copy-start(pred[4]{0:T(512)(128)(4,1)S(1)} %get-tuple-element.43) | copy-start | bytes 16
  418.5 67.7 %copy-start.14 = (pred[4]{0:T(512)(128)(4,1)}, pred[4]{0:T(512)(128)(4,1)S(1)}, u32[]{:S(2)}) copy-start(pred[4]{0:T(512)(128)(4,1)S(1)} %get-tuple-element.44) | copy-start | bytes 16
  489.0 35.6 %copy-start.3 = (bf16[192,720]{1,0:T(8,128)(2,1)S(1)}, bf16[192,720]{1,0:T(8,128)(2,1)}, u32[]{:S(2)}) copy-start(bf16[192,720]{1,0:T(8,128)(2,1)} %fusion.63) | copy-start | bytes 829444
  489.0 35.6 %copy-start.4 = (bf16[192,720]{1,0:T(8,128)(2,1)S(1)}, bf16[192,720]{1,0:T(8,128)(2,1)}, u32[]{:S(2)}) copy-start(bf16[192,720]{1,0:T(8,128)(2,1)} %fusion.62) | copy-start | bytes 829444
  491.6 37.1 %copy-start.11 = (f32[2880]{0:T(1024)S(1)}, f32[2880]{0:T(1024)}, u32[]{:S(2)}) copy-start(f32[2880]{0:T(1024)} %param.40) | copy-start | bytes 34564
  525.7 16.8 %copy-start.1 = (bf16[512,2880]{0,1:T(8,128)(2,1)S(1)}, bf16[512,2880]{0,1:T(8,128)(2,1)}, u32[]{:S(2)}) copy-start(bf16[512,2880]{0,1:T(8,128)(2,1)} %param.31) | copy-start | bytes 8847364
Sparse Core Ops, SparseCore 0:
  9.6 50.7 all-gather.6
  87.5 38.2 reduce-scatter.12
  129.0 29.5 all-gather.10
  174.5 38.9 reduce-scatter.14
  216.8 29.5 all-gather.8
  418.4 33.2 reduce-scatter.16
  491.7 31.0 reduce-scatter.18
where the time goes:
time: 559 us; the launch traced here: 550 us
  waiting for transfers between devices  338 us (60%)
  matrix products  97.5 us (17%)
  local copies, waits for them, and re-layouts  50.3 us (9%)
  starting transfers between devices  19.9 us (4%)
  other arithmetic  19.2 us (3%)
  between operations  15 us (3%)
  blocking collectives  9.24 us (2%)
    unnamed x11, waiting for transfers between devices  139 us
    all_to_all x2, waiting for transfers between devices, shards(): lax.all_to_all(shares_out, 'expert', split_axis=0, concat_axis=0, tiled=T...  66.1 us
    all_gather x1, waiting for transfers between devices, shards(): gathered_rows = lax.all_gather(hidden, 'dp', axis=1, tiled=True)  46.6 us
    all_gather x2, waiting for transfers between devices, shards(): column_h = lax.all_gather(resid_h, 'dp', axis=1, tiled=True)  45 us
    all_to_all x2, waiting for transfers between devices, shards(): lax.all_to_all(outgoing, 'expert', split_axis=0, concat_axis=0, tiled=True)  41.6 us
    dot_general x2, matrix products, shards(): jnp.dot(activated, down_weight, preferred_element_type=jnp.float32)  33.7 us
    dot_general x2, matrix products, shards(): up_part = jnp.dot(rows_in, up_weight, preferred_element_type=jnp.float32)  20.7 us
    unnamed x49, local copies, waits for them, and re-layouts  12.3 us
  transfers between devices with their start and end apart: 11, of which 10 were waited for; matrix products, arithmetic and copies ran while one was open for 18% of the time, Pallas kernels for 0%

commit v1 on v0

--- a/solution.py
+++ b/solution.py
@@ -98,7 +98,12 @@
     segment_row = segments[0]
     adapter_row = request_adapter[0]
     col_tokens = segment_row.shape[0]
-    gathered_rows = lax.all_gather(hidden, "dp", axis=1, tiled=True)
+    ring = [hidden]
+    for hop in range(3):
+        ring.append(lax.ppermute(ring[-1], "dp", [(dev, (dev + 1) % 4) for dev in range(4)]))
+    gathered_rows = jnp.roll(
+        jnp.concatenate(ring[::-1], axis=1), (lax.axis_index("dp") + 1) * ring[0].shape[1], axis=1
+    )
     width = gathered_rows.shape[1]
     normalized_hidden = rms_scale(gathered_rows.astype(jnp.float32), attention_gain).astype(
         jnp.bfloat16

time: 559 us -> 568 us (1.016)
  waiting for transfers between devices: 338 us -> 325 us
  local copies, waits for them, and re-layouts: 50.3 us -> 60.2 us
    all_gather x1 -> x0, waiting for transfers between devices: 46.6 us -> none  [shards(): gathered_rows = lax.all_gather(hidden, 'dp', axis=1, tiled=True)]
    ppermute x0 -> x3, waiting for transfers between devices: none -> 34.7 us  [shards(): lax.ppermute(ring[-1], 'dp', [(dev, (dev + 1) % 4) for dev in range(4)])]
    unnamed x49 -> x74, local copies, waits for them, and re-layouts: 12.3 us -> 19.5 us
    unnamed x11 -> x10, waiting for transfers between devices: 139 us -> 138 us
  transfers between devices with their start and end apart: 11 -> 13, of which waited for: 10 -> 12; matrix products, arithmetic and copies ran while one was open for 18% -> 19% of each run, Pallas kernels for 0% -> 0%
where the time goes in v1:
time: 568 us; the launch traced here: 557 us
  waiting for transfers between devices  325 us (57%)
  matrix products  100 us (18%)
  local copies, waits for them, and re-layouts  60.2 us (11%)
  other arithmetic  24.6 us (4%)
  starting transfers between devices  22.9 us (4%)
  between operations  15.2 us (3%)
  blocking collectives  9.22 us (2%)
    unnamed x10, waiting for transfers between devices  138 us
    all_to_all x2, waiting for transfers between devices, shards(): lax.all_to_all(shares_out, 'expert', split_axis=0, concat_axis=0, tiled=T...  66.1 us
    all_gather x2, waiting for transfers between devices, shards(): column_h = lax.all_gather(resid_h, 'dp', axis=1, tiled=True)  45.1 us
    all_to_all x2, waiting for transfers between devices, shards(): lax.all_to_all(outgoing, 'expert', split_axis=0, concat_axis=0, tiled=True)  41.6 us
    ppermute x3, waiting for transfers between devices, shards(): lax.ppermute(ring[-1], 'dp', [(dev, (dev + 1) % 4) for dev in range(4)])  34.7 us
    dot_general x2, matrix products, shards(): jnp.dot(activated, down_weight, preferred_element_type=jnp.float32)  33.7 us
    dot_general x2, matrix products, shards(): up_part = jnp.dot(rows_in, up_weight, preferred_element_type=jnp.float32)  20.7 us
    unnamed x74, local copies, waits for them, and re-layouts  19.5 us
  transfers between devices with their start and end apart: 13, of which 12 were waited for; matrix products, arithmetic and copies ran while one was open for 19% of the time, Pallas kernels for 0%

profile of v1, /device:TPU:0, one launch (start us, length us, event | category | flops | bytes accessed | tf_op | source)
XLA Modules:
  0.0 557.3 jit_solution(14895301659038421166)
XLA Ops:
  7.2 3.1 collective-permute-start
  15.8 9.4 %collective-permute-done = bf16[384,720]{0,1:T(8,128)(2,1)} collective-permute-done((bf16[384,720]{0,1:T(8,128)(2,1)}, bf16[384,720]{0,1:T(8,128)(2,1)}, u32[]{:S(2)}, u32[]{:S(2)}) %collective-permute-start) | collective-permute-done | bytes 552992 | tf_op jit(solution)/shard_map/ppermute | solution.py:103
  28.1 12.8 %collective-permute-done.1 = bf16[384,720]{0,1:T(8,128)(2,1)S(1)} collective-permute-done((bf16[384,720]{0,1:T(8,128)(2,1)}, bf16[384,720]{0,1:T(8,128)(2,1)S(1)}, u32[]{:S(2)}, u32[]{:S(2)}) %collective-permute-start.1) | collective-permute-done | bytes 552992 | tf_op jit(solution)/shard_map/ppermute | solution.py:103
  43.1 12.4 %collective-permute-done.2 = bf16[384,720]{0,1:T(8,128)(2,1)S(1)} collective-permute-done((bf16[384,720]{0,1:T(8,128)(2,1)S(1)}, bf16[384,720]{0,1:T(8,128)(2,1)S(1)}, u32[]{:S(2)}, u32[]{:S(2)}) %collective-permute-start.2) | collective-permute-done | bytes 552992 | tf_op jit(solution)/shard_map/ppermute | solution.py:103
  58.4 2.0 copy-done.5
  61.7 4.7 convolution_multiply_fusion
  66.4 6.2 %fusion.56 = f32[384,640]{1,0:T(8,128)} fusion(f32[384,640]{1,0:T(8,128)} %convolution_multiply_fusion, bf16[2880,1,640]{2,0,1:T(8,128)(2,1)} %param.29, f32[2880]{0:T(1024)} %param.28, f32[384]{0:T(512)} %add_rsqrt_fusion, bf16[384,5760]{0,1:T(8,128)(2,1)} %copy-done.5, s32[]{:T(128)S(6)} %select_n.116), kind=kOutput, calls=%fused_computation.65 | convolution fusion | flops 1420247040 | bytes 7878660 | tf_op jit(solution)/shard_map/dot_general | solution.py:111
  72.6 2.5 copy.64
  79.1 2.2 fusion.19
  81.4 2.3 fusion.61
  87.0 2.7 convolution_convert_fusion.4
  90.1 2.9 fusion.141
  94.0 36.3 %reduce-scatter.13.cloned.1.call-done = bf16[896,192]{1,0:T(8,128)(2,1)} async-done(((bf16[3584,192]{1,0:T(8,128)(2,1)}), bf16[896,192]{1,0:T(8,128)(2,1)}) %reduce-scatter.13.cloned.1.call-update) | async-done | bytes 344080
  137.2 3.4 scatter_custom_fusion.1
  140.6 22.6 %all-gather.8.cloned.1.call-done = bf16[4,720,192]{1,2,0:T(8,128)(2,1)} async-done(((bf16[1,720,192]{1,2,0:T(8,128)(2,1)}), bf16[4,720,192]{1,2,0:T(8,128)(2,1)}) %all-gather.8.cloned.1.call-update) | async-done | bytes 1105936 | tf_op jit(solution)/shard_map/all_gather | solution.py:208
  163.2 2.2 copy.75
  167.0 4.4 convolution_convert_fusion.1
  171.5 4.7 all-to-all-start
  177.2 41.2 %reduce-scatter.15.cloned.1.call-done = bf16[896,192]{1,0:T(8,128)(2,1)} async-done(((bf16[3584,192]{1,0:T(8,128)(2,1)}), bf16[896,192]{1,0:T(8,128)(2,1)}) %reduce-scatter.15.cloned.1.call-update) | async-done | bytes 344080
  225.2 3.6 scatter_custom_fusion
  228.8 22.4 %all-gather.6.cloned.1.call-done = bf16[4,720,192]{1,2,0:T(8,128)(2,1)} async-done(((bf16[1,720,192]{1,2,0:T(8,128)(2,1)}), bf16[4,720,192]{1,2,0:T(8,128)(2,1)}) %all-gather.6.cloned.1.call-update) | async-done | bytes 1105936 | tf_op jit(solution)/shard_map/all_gather | solution.py:208
  251.2 3.2 copy.72
  254.4 2.7 reshape.552
  257.8 4.4 convolution_convert_fusion
  262.2 4.7 all-to-all-start.1
  266.9 10.4 %fusion.4 = f32[1024,720]{0,1:T(8,128)} fusion(bf16[1024,2944]{1,0:T(8,128)(2,1)} %bitcast.45, bf16[1,2880,720]{1,2,0:T(8,128)(2,1)} %param.38), kind=kOutput, calls=%fused_computation.16 | convolution fusion | flops 4246732800 | bytes 13125632 | tf_op jit(solution)/shard_map/dot_general | solution.py:239
  277.3 16.8 %convolution_convert_fusion.2 = bf16[1024,2944]{1,0:T(8,128)(2,1)} fusion(bf16[720,2880]{1,0:T(8,128)(2,1)} %bitcast.185, f32[1024,720]{0,1:T(8,128)} %fusion.4, bf16[1,2880,720]{1,2,0:T(8,128)(2,1)} %param.37, bf16[1024,2944]{1,0:T(8,128)(2,1)} %bitcast.45), kind=kOutput, calls=%fused_computation.12 | convolution fusion | flops 8596750336 | bytes 23302144 | tf_op jit(solution)/shard_map/dot_general | solution.py:244
  294.1 41.6 %all-to-all-done.1 = bf16[8,128,2944]{2,1,0:T(8,128)(2,1)} async-done(((bf16[8,128,2944]{2,1,0:T(8,128)(2,1)}), bf16[8,128,2944]{2,1,0:T(8,128)(2,1)}, u32[]{:S(2)}, u32[]{:S(2)}) %all-to-all-start.1) | async-done | bytes 6029344 | tf_op jit(solution)/shard_map/all_to_all | solution.py:232
  335.7 4.9 all-to-all-start.3
  340.7 10.4 %fusion.8 = f32[1024,720]{0,1:T(8,128)} fusion(bf16[1024,2944]{1,0:T(8,128)(2,1)} %bitcast.40, bf16[1,2880,720]{1,2,0:T(8,128)(2,1)} %param.38), kind=kOutput, calls=%fused_computation.20 | convolution fusion | flops 4246732800 | bytes 13125632 | tf_op jit(solution)/shard_map/dot_general | solution.py:239
  351.1 16.8 %convolution_convert_fusion.3 = bf16[1024,2944]{1,0:T(8,128)(2,1)} fusion(bf16[720,2880]{1,0:T(8,128)(2,1)} %bitcast.186, f32[1024,720]{0,1:T(8,128)} %fusion.8, bf16[1,2880,720]{1,2,0:T(8,128)(2,1)} %param.37, bf16[1024,2944]{1,0:T(8,128)(2,1)} %bitcast.40), kind=kOutput, calls=%fused_computation.13 | convolution fusion | flops 8596750336 | bytes 23302144 | tf_op jit(solution)/shard_map/dot_general | solution.py:244
  367.9 41.6 %all-to-all-done.3 = bf16[8,128,2944]{2,1,0:T(8,128)(2,1)} async-done(((bf16[8,128,2944]{2,1,0:T(8,128)(2,1)}), bf16[8,128,2944]{2,1,0:T(8,128)(2,1)}, u32[]{:S(2)}, u32[]{:S(2)}) %all-to-all-start.3) | async-done | bytes 6029344 | tf_op jit(solution)/shard_map/all_to_all | solution.py:248
  409.5 4.7 all-to-all-start.2
  414.8 5.8 %fusion.145 = (bf16[192,2880]{1,0:T(8,128)(2,1)}, f32[192,2880]{1,0:T(8,128)}) fusion(bf16[192,1024]{1,0:T(8,128)(2,1)S(1)} %fusion.51, bf16[1024,2944]{1,0:T(8,128)(2,1)} %bitcast.47), kind=kOutput, calls=%fused_computation.228 | convolution fusion | flops 1133015040 | bytes 9740288 | tf_op jit(solution)/shard_map/dot_general | solution.py:262
  420.6 2.5 copy.88
  423.9 2.2 gather_fusion
  426.1 30.4 %reduce-scatter.17.cloned.1.call-done = bf16[720,192]{1,0:T(8,128)(2,1)} async-done(((bf16[2880,192]{1,0:T(8,128)(2,1)}), bf16[720,192]{1,0:T(8,128)(2,1)}) %reduce-scatter.17.cloned.1.call-update) | async-done | bytes 276496
  456.6 1.8 copy.89
  458.4 24.6 %all-to-all-done.2 = bf16[8,128,2944]{2,1,0:T(8,128)(2,1)} async-done(((bf16[8,128,2944]{2,1,0:T(8,128)(2,1)}), bf16[8,128,2944]{2,1,0:T(8,128)(2,1)}, u32[]{:S(2)}, u32[]{:S(2)}) %all-to-all-start.2) | async-done | bytes 6029344 | tf_op jit(solution)/shard_map/all_to_all | solution.py:248
  483.0 5.8 %fusion.146 = (bf16[192,2880]{1,0:T(8,128)(2,1)}, f32[192,2880]{1,0:T(8,128)}) fusion(bf16[192,1024]{1,0:T(8,128)(2,1)S(1)} %fusion.50, bf16[1024,2944]{1,0:T(8,128)(2,1)} %bitcast.48), kind=kOutput, calls=%fused_computation.229 | convolution fusion | flops 1133015040 | bytes 9740288 | tf_op jit(solution)/shard_map/dot_general | solution.py:262
  488.8 2.2 gather_fusion.1
  491.5 2.4 pad_maximum_fusion.1
  493.9 2.5 copy.90
  498.8 28.9 %reduce-scatter.19.cloned.1.call-done = bf16[720,208]{1,0:T(8,128)(2,1)} async-done(((bf16[2880,208]{1,0:T(8,128)(2,1)}), bf16[720,208]{1,0:T(8,128)(2,1)}) %reduce-scatter.19.cloned.1.call-update) | async-done | bytes 299536
  530.2 2.2 add_convert_fusion
  532.4 2.1 copy.80
  536.4 9.2 %all-gather.2 = bf16[8,4,2880]{2,1,0:T(4,128)(2,1)S(1)} all-gather(bf16[1,4,2880]{2,1,0:T(4,128)(2,1)S(1)} %fusion.110), channel_id=1, replica_groups=mesh['dp'=4,'expert'=8] {'expert'}, dimensions={0}, use_global_device_ids=true | all-gather | bytes 207360 | tf_op jit(solution)/shard_map/all_gather | solution.py:291
  545.7 4.4 fusion.147
  (178 shorter events, 48.7 us)
Async XLA Ops:
  7.2 79.8 %copy-start = (bf16[512,2880]{0,1:T(8,128)(2,1)S(1)}, bf16[512,2880]{0,1:T(8,128)(2,1)}, u32[]{:S(2)}) copy-start(bf16[512,2880]{0,1:T(8,128)(2,1)} %param.31) | copy-start | bytes 8847364
  7.2 49.7 %copy-start.2 = (bf16[384,720]{0,1:T(8,128)(2,1)S(1)}, bf16[384,720]{0,1:T(8,128)(2,1)}, u32[]{:S(2)}) copy-start(bf16[384,720]{0,1:T(8,128)(2,1)} %param.23) | copy-start | bytes 1658884
  7.2 123.1 %reduce-scatter.13.cloned.1.call-start = ((), (), s32[]{:S(2)}) async-start(), calls=%async_computation.10 | async-start | bytes 2293760
  7.2 18.0 %collective-permute-start = (bf16[384,720]{0,1:T(8,128)(2,1)}, bf16[384,720]{0,1:T(8,128)(2,1)}, u32[]{:S(2)}, u32[]{:S(2)}) collective-permute-start(bf16[384,720]{0,1:T(8,128)(2,1)} %param.23), channel_id=1, source_target_pairs={{0,8},{8,16},{16,24},{24,0},{1,9},{9,17},{17,25},{25,1},{2,10},{10... | collective-permute-start | bytes 1658888 | tf_op jit(solution)/shard_map/ppermute | solution.py:103
  13.5 1.4 copy-start.17
  15.8 25.2 %copy-start.12 = (bf16[384,48]{0,1:T(8,128)(2,1)}, bf16[384,48]{0,1:T(8,128)(2,1)S(1)}, u32[]{:S(2)}) copy-start(bf16[384,48]{0,1:T(8,128)(2,1)S(1)} %dynamic_update_slice.5) | copy-start | bytes 110596
  25.2 15.7 %collective-permute-start.1 = (bf16[384,720]{0,1:T(8,128)(2,1)}, bf16[384,720]{0,1:T(8,128)(2,1)S(1)}, u32[]{:S(2)}, u32[]{:S(2)}) collective-permute-start(bf16[384,720]{0,1:T(8,128)(2,1)} %collective-permute-done), channel_id=1, source_target_pairs={{0,8},{8,16},{16,24},{24,0},{1,9},{9,17},{17,25},{25,1},{2,10},{10... | collective-permute-start | bytes 1658888 | tf_op jit(solution)/shard_map/ppermute | solution.py:103
  25.2 17.9 %copy-start.23 = (f32[32]{0:T(128)}, f32[32]{0:T(128)S(1)}, u32[]{:S(2)}) copy-start(f32[32]{0:T(128)S(1)} %multiply_power_fusion) | copy-start | bytes 388
  28.1 15.0 %copy-start.16 = (f32[384]{0:T(512)}, f32[384]{0:T(512)S(1)}, u32[]{:S(2)}) copy-start(f32[384]{0:T(512)S(1)} %fusion.119) | copy-start | bytes 4612
  40.9 14.6 %collective-permute-start.2 = (bf16[384,720]{0,1:T(8,128)(2,1)S(1)}, bf16[384,720]{0,1:T(8,128)(2,1)S(1)}, u32[]{:S(2)}, u32[]{:S(2)}) collective-permute-start(bf16[384,720]{0,1:T(8,128)(2,1)S(1)} %collective-permute-done.1), channel_id=1, source_target_pairs={{0,8},{8,16},{16,24},{24,0},{1,9},{9,17},{17,25},{25,1},{2,10},{10... | collective-permute-start | bytes 1658888 | tf_op jit(solution)/shard_map/ppermute | solution.py:103
  58.4 2.0 copy-start.5
  78.1 3.2 copy-start.25
  78.1 3.3 copy-start.11
  81.4 3.0 copy-start.14
  83.6 0.8 copy-start.9
  87.0 2.7 copy-start.13
  87.0 2.8 copy-start.10
  93.0 0.9 copy-start.19
  93.0 0.9 copy-start.24
  93.0 39.4 %copy-start.7 = (bf16[128,720]{0,1:T(8,128)(2,1)S(1)}, bf16[128,720]{0,1:T(8,128)(2,1)}, u32[]{:S(2)}) copy-start(bf16[128,720]{0,1:T(8,128)(2,1)} %param.35) | copy-start | bytes 552964
  93.0 70.2 %all-gather.8.cloned.1.call-start = ((), (), s32[]{:S(2)}) async-start(), calls=%async_computation.9 | async-start | bytes 1474560 | tf_op jit(solution)/shard_map/all_gather | solution.py:208
  133.4 33.3 %copy-start.15 = (f32[2880]{0:T(1024)S(1)}, f32[2880]{0:T(1024)}, u32[]{:S(2)}) copy-start(f32[2880]{0:T(1024)} %param.36) | copy-start | bytes 34564
  171.5 85.7 %all-to-all-start = ((bf16[8,128,2944]{2,1,0:T(8,128)(2,1)}), bf16[8,128,2944]{2,1,0:T(8,128)(2,1)}, u32[]{:S(2)}, u32[]{:S(2)}) async-start(bf16[8,128,2944]{2,1,0:T(8,128)(2,1)} %bitcast.151), calls=%async_computation | async-start | bytes 12058624 | tf_op jit(solution)/shard_map/all_to_all | solution.py:232
  176.2 44.3 %copy-start.8 = (bf16[128,720]{0,1:T(8,128)(2,1)S(1)}, bf16[128,720]{0,1:T(8,128)(2,1)}, u32[]{:S(2)}) copy-start(bf16[128,720]{0,1:T(8,128)(2,1)} %param.35) | copy-start | bytes 552964
  176.2 42.1 %reduce-scatter.15.cloned.1.call-start = ((), (), s32[]{:S(2)}) async-start(), calls=%async_computation.11 | async-start | bytes 2293760
  176.9 74.3 %all-gather.6.cloned.1.call-start = ((), (), s32[]{:S(2)}) async-start(), calls=%async_computation.8 | async-start | bytes 1474560 | tf_op jit(solution)/shard_map/all_gather | solution.py:208
  262.2 73.5 %all-to-all-start.1 = ((bf16[8,128,2944]{2,1,0:T(8,128)(2,1)}), bf16[8,128,2944]{2,1,0:T(8,128)(2,1)}, u32[]{:S(2)}, u32[]{:S(2)}) async-start(bf16[8,128,2944]{2,1,0:T(8,128)(2,1)} %bitcast.152), calls=%async_computation.1 | async-start | bytes 12058624 | tf_op jit(solution)/shard_map/all_to_all | solution.py:232
  335.7 73.7 %all-to-all-start.3 = ((bf16[8,128,2944]{2,1,0:T(8,128)(2,1)}), bf16[8,128,2944]{2,1,0:T(8,128)(2,1)}, u32[]{:S(2)}, u32[]{:S(2)}) async-start(bf16[8,128,2944]{2,1,0:T(8,128)(2,1)} %bitcast.160), calls=%async_computation.3 | async-start | bytes 12058624 | tf_op jit(solution)/shard_map/all_to_all | solution.py:248
  409.5 73.5 %all-to-all-start.2 = ((bf16[8,128,2944]{2,1,0:T(8,128)(2,1)}), bf16[8,128,2944]{2,1,0:T(8,128)(2,1)}, u32[]{:S(2)}, u32[]{:S(2)}) async-start(bf16[8,128,2944]{2,1,0:T(8,128)(2,1)} %bitcast.159), calls=%async_computation.2 | async-start | bytes 12058624 | tf_op jit(solution)/shard_map/all_to_all | solution.py:248
  414.2 42.4 %reduce-scatter.17.cloned.1.call-start = ((), (), s32[]{:S(2)}) async-start(), calls=%async_computation.12 | async-start | bytes 1843200
  423.2 104.5 %reduce-scatter.19.cloned.1.call-start = ((), (), s32[]{:S(2)}) async-start(), calls=%async_computation.13 | async-start | bytes 1843200
  423.3 67.7 %copy-start.20 = (pred[4]{0:T(512)(128)(4,1)}, pred[4]{0:T(512)(128)(4,1)S(1)}, u32[]{:S(2)}) copy-start(pred[4]{0:T(512)(128)(4,1)S(1)} %get-tuple-element.42) | copy-start | bytes 16
  423.4 67.7 %copy-start.21 = (pred[4]{0:T(512)(128)(4,1)}, pred[4]{0:T(512)(128)(4,1)S(1)}, u32[]{:S(2)}) copy-start(pred[4]{0:T(512)(128)(4,1)S(1)} %get-tuple-element.43) | copy-start | bytes 16
  423.4 67.7 %copy-start.22 = (pred[4]{0:T(512)(128)(4,1)}, pred[4]{0:T(512)(128)(4,1)S(1)}, u32[]{:S(2)}) copy-start(pred[4]{0:T(512)(128)(4,1)S(1)} %get-tuple-element.44) | copy-start | bytes 16
  491.5 38.7 %copy-start.3 = (bf16[192,720]{1,0:T(8,128)(2,1)S(1)}, bf16[192,720]{1,0:T(8,128)(2,1)}, u32[]{:S(2)}) copy-start(bf16[192,720]{1,0:T(8,128)(2,1)} %fusion.65) | copy-start | bytes 829444
  491.5 38.7 %copy-start.4 = (bf16[192,720]{1,0:T(8,128)(2,1)S(1)}, bf16[192,720]{1,0:T(8,128)(2,1)}, u32[]{:S(2)}) copy-start(bf16[192,720]{1,0:T(8,128)(2,1)} %fusion.64) | copy-start | bytes 829444
  493.9 42.4 %copy-start.18 = (f32[2880]{0:T(1024)S(1)}, f32[2880]{0:T(1024)}, u32[]{:S(2)}) copy-start(f32[2880]{0:T(1024)} %param.40) | copy-start | bytes 34564
  528.8 0.7 copy-start.6
  530.2 19.9 %copy-start.1 = (bf16[512,2880]{0,1:T(8,128)(2,1)S(1)}, bf16[512,2880]{0,1:T(8,128)(2,1)}, u32[]{:S(2)}) copy-start(bf16[512,2880]{0,1:T(8,128)(2,1)} %param.31) | copy-start | bytes 8847364
Sparse Core Ops, SparseCore 0:
  93.1 37.1 reduce-scatter.12
  133.6 29.5 all-gather.7
  179.3 38.9 reduce-scatter.14
  221.6 29.5 all-gather.5
  423.3 33.2 reduce-scatter.16
  496.6 31.0 reduce-scatter.18
